TPU v7x, 32 devices: a whole 2x2x4 slice. The times are simulated.
32 devices in a mesh: tm: 2 (over x), prow: 4 (over z), pcol: 4 (over y, core).
Axes of the slice: x: 2, y: 2, z: 4, core: 2. Of those that a mesh axis runs over, the one named last changes fastest.
Arguments:
- signal: bfloat16 [2048, 15360], P(('prow', 'pcol'), 'tm'), may hold values from -8 to 8
- offsets: int32 [4], replicated, may hold values from 0 to 511, as said below
- pair_list: int32 [4, 4, 4, 2], P('prow', 'pcol'), may hold values from 0 to 3, as said below
Outputs:
- correlations: bfloat16 [4, 4, 4, 128, 128, 256], P('prow', 'pcol', None, 'tm')
Inputs may be any that keep to these rules, and one draw needn't show every extreme that they name: `offsets`: some window has the largest offset. `pair_list`: entry (a, b) of cell (r, c) pairs row block r n + a with column block b n + c, n the number of devices of pcol, and the row block's number is never above the column block's; pairs may repeat.
All inputs are finite; a program needn't handle non-finite values.
Results may differ from a plain program's by a relative error of at most 0.0058.
Values may be sent and summed in bfloat16 or wider, within the bound.
No kernel may reach another device: no remote copies, remote signals or barrier semaphores. Data moves between devices by JAX's collectives and lax.ppermute only.
A program may use at most 128 MiB of HBM per device.

v0:
```python
import math
import jax
import jax.numpy as jnp
from jax import lax
from jax.sharding import PartitionSpec as P

WIN = 7680
NF = 384
K0 = 32
LAGS = 256
SPAN = 4
NP = 4
STEP = 3840
HALO = 4352
two_pi = 2.0 * math.pi


def from_behind(value, axis, steps):
    count = lax.axis_size(axis)
    initial, last = (max(0, -steps), min(count, count - steps))
    return lax.ppermute(value, axis, [(source, source + steps) for source in range(initial, last)])


def forward_table():
    sample_idx = jnp.arange(WIN, dtype=jnp.int32)
    freq_bins = K0 + jnp.arange(NF, dtype=jnp.int32)
    wrapped = sample_idx[:, None] * freq_bins[None, :] % WIN
    phase_angle = wrapped.astype(jnp.float32) * (two_pi / WIN)
    taper_curve = 0.5 - 0.5 * jnp.cos(sample_idx.astype(jnp.float32) * (two_pi / WIN))
    cosine = taper_curve[:, None] * jnp.cos(phase_angle)
    sine = -taper_curve[:, None] * jnp.sin(phase_angle)
    return jnp.concatenate([cosine, sine], axis=1).astype(jnp.bfloat16)


def lag_table(count):
    freq_bins = K0 + jnp.arange(NF, dtype=jnp.int32)
    shifted = (jnp.arange(LAGS, dtype=jnp.int32) - LAGS // 2) % WIN
    wrapped = freq_bins[:, None] * shifted[None, :] % WIN
    phase_angle = wrapped.astype(jnp.float32) * (two_pi / WIN)
    factor = 1.0 / math.sqrt(NF * count)
    return jnp.concatenate(
        [jnp.cos(phase_angle) * factor, -jnp.sin(phase_angle) * factor], axis=0
    ).astype(jnp.bfloat16)


def whiten(spectra):
    real_part = spectra[..., :NF]
    imag_part = spectra[..., NF:]
    power_sum = real_part * real_part + imag_part * imag_part
    freq_bins = jnp.arange(NF, dtype=jnp.int32)
    band_matrix = (jnp.abs(freq_bins[:, None] - freq_bins[None, :]) <= SPAN).astype(jnp.float32)
    smooth = jnp.einsum(
        "...f,fg->...g", power_sum, band_matrix, precision=lax.Precision.HIGHEST
    ) / (2 * SPAN + 1)
    water_level = jnp.mean(power_sum, axis=-1, keepdims=True)
    weight = lax.rsqrt(smooth + 0.5 * water_level + 1e-06)
    return (spectra * jnp.concatenate([weight, weight], axis=-1)).astype(jnp.bfloat16)


def cross_pair(row_block, col_block, lags):
    row_real = row_block[..., :NF]
    row_imag = row_block[..., NF:]
    col_both = jnp.concatenate([col_block[..., :NF], col_block[..., NF:]], axis=0)
    row_first = jnp.concatenate([row_real, row_imag], axis=0)
    row_second = jnp.concatenate([row_imag, -row_real], axis=0)
    real_sum = jnp.einsum("wif,wjf->ijf", row_first, col_both, preferred_element_type=jnp.float32)
    imag_sum = jnp.einsum("wif,wjf->ijf", row_second, col_both, preferred_element_type=jnp.float32)
    cross = jnp.concatenate([real_sum, imag_sum], axis=-1).astype(jnp.bfloat16)
    flat = cross.reshape(-1, 2 * NF)
    result = jnp.dot(flat, lags, preferred_element_type=jnp.float32).astype(jnp.bfloat16)
    return result.reshape(row_block.shape[1], col_block.shape[1], LAGS)


def on_device(signal, offsets, pair_list):
    channels_here = signal.shape[0]
    samples_here = signal.shape[1]
    w_dev = samples_here // STEP
    n_tm = lax.axis_size("tm")
    tm_index = lax.axis_index("tm")
    dft_table = forward_table()
    head_samples = signal[:, :HALO]
    next_head = from_behind(head_samples, "tm", -1)
    extended = jnp.concatenate([signal, next_head], axis=1)

    def one_window(window):
        first_sample = window * STEP + offsets[tm_index * w_dev + window]
        segment = lax.dynamic_slice_in_dim(extended, first_sample, WIN, 1)
        return jnp.dot(segment, dft_table, preferred_element_type=jnp.float32)

    spectra = lax.map(one_window, jnp.arange(w_dev, dtype=jnp.int32))
    whitened = whiten(spectra)
    own_piece = whitened[None]
    row_gathered = lax.all_gather(own_piece, ("tm", "pcol"), axis=0, tiled=True)
    col_gathered = lax.all_gather(own_piece, ("tm", "prow"), axis=0, tiled=True)
    row_gathered = row_gathered.reshape(n_tm, -1, w_dev, channels_here, 2 * NF)
    col_gathered = col_gathered.reshape(n_tm, -1, w_dev, channels_here, 2 * NF)
    pick_dim = 1
    lags = lag_table(n_tm * w_dev)
    local_pairs = pair_list[0, 0]
    half_rows = channels_here // n_tm
    first_row = tm_index * half_rows

    def one_pair(pair_index):
        row_pick = local_pairs[pair_index, 0]
        col_pick = local_pairs[pair_index, 1]
        row_whole = lax.dynamic_index_in_dim(row_gathered, row_pick, pick_dim, keepdims=False)
        col_whole = lax.dynamic_index_in_dim(col_gathered, col_pick, pick_dim, keepdims=False)
        row_whole = row_whole.reshape(n_tm * w_dev, channels_here, 2 * NF)
        col_whole = col_whole.reshape(n_tm * w_dev, channels_here, 2 * NF)
        row_block = lax.dynamic_slice_in_dim(row_whole, first_row, half_rows, 1)
        return cross_pair(row_block, col_whole, lags)

    result = lax.map(one_pair, jnp.arange(NP, dtype=jnp.int32))
    return result.reshape(1, 1, NP, half_rows, channels_here, LAGS)


def solution(mesh):
    placed = (P(("prow", "pcol"), "tm"), P(), P("prow", "pcol", None, None))
    return jax.shard_map(
        on_device,
        mesh=mesh,
        in_specs=placed,
        out_specs=P("prow", "pcol", None, "tm", None, None),
        check_vma=False,
    )
```

profile of v0, /device:TPU:0, one launch (start us, length us, event | category | flops | bytes accessed | tf_op | source)
XLA Modules:
  0.0 409.1 jit_solution(12209533261240623052)
XLA Ops:
  6.5 1.3 slice.29
  7.9 1.3 collective-permute-start
  9.3 52.4 %multiply_convert_fusion.1 = (bf16[7680,384]{1,0:T(8,128)(2,1)S(1)}, bf16[7680,384]{1,0:T(8,128)(2,1)S(1)}) fusion(s32[384]{0:T(512)S(1)} %iota_add_fusion, f32[7680]{0:T(1024)S(1)} %get-tuple-element.245, f32[7680]{0:T(1024)S(1)} %get-tuple-element.246), kind=kLoop, calls=%fused_computation.36 | loop fusion | flops 38338560 | bytes 11859456 | tf_op jit(solution)/shard_map/convert.8
  61.8 5.0 %pad_maximum_fusion.3 = bf16[7680,768]{1,0:T(8,128)(2,1)} fusion(bf16[7680,384]{1,0:T(8,128)(2,1)S(1)} %get-tuple-element.244, bf16[7680,384]{1,0:T(8,128)(2,1)S(1)} %get-tuple-element.243), kind=kLoop, calls=%fused_computation.34 | loop fusion | flops 23592960 | bytes 23592960 | tf_op jit(solution)/shard_map/concatenate | solution.py:32
  66.7 1.4 pad_maximum_fusion.4
  68.2 19.9 %while.24 = (s32[]{:T(128)}, f32[2,128,768]{2,1,0:T(8,128)}, s32[2]{0:T(128)S(1)}, s32[]{:T(128)}, s32[4]{0:T(128)S(1)}, /*index=5*/bf16[128,12032]{1,0:T(8,128)...) while((s32[]{:T(128)}, f32[2,128,768]{2,1,0:T(8,128)}, ...), condition=%wide.region_1.2_spmd, body=%wide.region_0.1_spmd.sunk | while | flops 1509949440 | bytes 14156537 | solution.py:90
  68.2 0.6 dynamic_slice.65
  71.2 7.0 %fusion.61 = f32[2,128,768]{2,1,0:T(8,128)} fusion(f32[2,128,768]{2,1,0:T(8,128)} %get-tuple-element.370, s32[]{:T(128)} %get-tuple-element.369, bf16[7680,768]{1,0:T(8,128)(2,1)} %get-tuple-element.387, bf16[128,12032]{1,0:T(8,128)(2,1)S(1)} %get-tuple-element.386, s32[]{:T(128)S(6)} %select_n.90), kind=kOutput, calls=%fused_computation.3.clone.1 | convolution fusion | flops 1509949440 | bytes 14156292 | tf_op jit(solution)/shard_map/while/body/eval_jaxpr/dot_general | solution.py:88
  78.2 0.6 dynamic_slice.65
  81.2 6.9 %fusion.61 = f32[2,128,768]{2,1,0:T(8,128)} fusion(f32[2,128,768]{2,1,0:T(8,128)} %get-tuple-element.370, s32[]{:T(128)} %get-tuple-element.369, bf16[7680,768]{1,0:T(8,128)(2,1)} %get-tuple-element.387, bf16[128,12032]{1,0:T(8,128)(2,1)S(1)} %get-tuple-element.386, s32[]{:T(128)S(6)} %select_n.90), kind=kOutput, calls=%fused_computation.3.clone.1 | convolution fusion | flops 1509949440 | bytes 14156292 | tf_op jit(solution)/shard_map/while/body/eval_jaxpr/dot_general | solution.py:88
  88.2 1.2 fusion.42
  89.4 1.7 fusion.32
  91.1 2.0 fusion.33
  93.2 0.7 all-gather.7.cloned.1.call-update
  93.9 2.0 multiply_convert_fusion.3
  95.9 62.2 %all-gather.5.cloned.1.call-done = bf16[16,128,768]{2,1,0:T(8,128)(2,1)} async-done(((bf16[2,128,768]{2,1,0:T(8,128)(2,1)}), bf16[16,128,768]{2,1,0:T(8,128)(2,1)}) %all-gather.5.cloned.1.call-update) | async-done | bytes 3145744 | tf_op jit(solution)/shard_map/all_gather | solution.py:94
  158.1 32.8 %all-gather.7.cloned.1.call-done = bf16[16,128,768]{2,1,0:T(8,128)(2,1)} async-done(((bf16[2,128,768]{2,1,0:T(8,128)(2,1)}), bf16[16,128,768]{2,1,0:T(8,128)(2,1)}) %all-gather.7.cloned.1.call-update) | async-done | bytes 3145744 | tf_op jit(solution)/shard_map/all_gather | solution.py:93
  190.9 211.1 %while.25 = (s32[]{:T(128)}, bf16[4,64,128,256]{3,2,1,0:T(8,128)(2,1)}, s32[4]{0:T(128)S(1)}, s32[4,2]{0,1:T(2,128)S(1)}, bf16[2,4,2,128,768]{4,3,2,1,0:T(8,128)...) while((s32[]{:T(128)}, ...), condition=%wide.region_4.5_spmd, body=%wide.region_3.4_spmd.sunk | while | flops 3360456704 | bytes 74515224 | solution.py:113
  212.0 0.6 dynamic_slice.69
  214.5 0.6 constant_dynamic-slice_fusion.9
  218.7 1.5 constant_dynamic-slice_fusion.10
  220.2 0.6 copy.20
  220.8 0.6 fusion.66
  221.4 0.6 copy.21
  222.3 2.2 convolution_convert_fusion.5
  224.5 12.5 %copy.23 = bf16[48,8,64,128]{3,1,2,0:T(8,128)(2,1)S(1)} copy(bf16[48,8,64,128]{3,2,1,0:T(8,128)(2,1)S(1)} %bitcast.66) | data formatting | bytes 12582912 | tf_op jit(solution)/shard_map/while
  237.0 2.2 convolution_convert_fusion.4
  239.1 12.5 %copy.22 = bf16[48,8,64,128]{3,1,2,0:T(8,128)(2,1)S(1)} copy(bf16[48,8,64,128]{3,2,1,0:T(8,128)(2,1)S(1)} %bitcast.65) | data formatting | bytes 12582912 | tf_op jit(solution)/shard_map/while
  251.6 5.6 %fusion.68 = bf16[8192,256]{1,0:T(8,128)(2,1)S(1)} fusion(bf16[768,256]{1,0:T(8,128)(2,1)S(1)} %get-tuple-element.424, bf16[8192,384]{0,1:T(8,128)(2,1)S(1)} %bitcast.68, bf16[8192,384]{0,1:T(8,128)(2,1)S(1)} %bitcast.67), kind=kOutput, calls=%fused_computation.9.clone.1 | convolution fusion | flops 3248488448 | bytes 17170432 | tf_op jit(solution)/shard_map/while/body/eval_jaxpr/dot_general | solution.py:70
  257.2 2.3 constant_dynamic-update-slice_fusion.2
  259.5 0.6 dynamic_slice.69
  262.0 0.6 constant_dynamic-slice_fusion.9
  266.2 1.5 constant_dynamic-slice_fusion.10
  267.7 0.6 copy.20
  268.3 0.6 fusion.66
  268.9 0.6 copy.21
  269.8 2.2 convolution_convert_fusion.5
  272.0 12.5 %copy.23 = bf16[48,8,64,128]{3,1,2,0:T(8,128)(2,1)S(1)} copy(bf16[48,8,64,128]{3,2,1,0:T(8,128)(2,1)S(1)} %bitcast.66) | data formatting | bytes 12582912 | tf_op jit(solution)/shard_map/while
  284.4 2.2 convolution_convert_fusion.4
  286.6 12.5 %copy.22 = bf16[48,8,64,128]{3,1,2,0:T(8,128)(2,1)S(1)} copy(bf16[48,8,64,128]{3,2,1,0:T(8,128)(2,1)S(1)} %bitcast.65) | data formatting | bytes 12582912 | tf_op jit(solution)/shard_map/while
  299.1 5.6 %fusion.68 = bf16[8192,256]{1,0:T(8,128)(2,1)S(1)} fusion(bf16[768,256]{1,0:T(8,128)(2,1)S(1)} %get-tuple-element.424, bf16[8192,384]{0,1:T(8,128)(2,1)S(1)} %bitcast.68, bf16[8192,384]{0,1:T(8,128)(2,1)S(1)} %bitcast.67), kind=kOutput, calls=%fused_computation.9.clone.1 | convolution fusion | flops 3248488448 | bytes 17170432 | tf_op jit(solution)/shard_map/while/body/eval_jaxpr/dot_general | solution.py:70
  304.7 2.3 constant_dynamic-update-slice_fusion.2
  307.0 0.6 dynamic_slice.69
  309.5 0.6 constant_dynamic-slice_fusion.9
  313.7 1.5 constant_dynamic-slice_fusion.10
  315.2 0.6 copy.20
  316.4 0.6 copy.21
  317.3 2.2 convolution_convert_fusion.5
  319.5 12.5 %copy.23 = bf16[48,8,64,128]{3,1,2,0:T(8,128)(2,1)S(1)} copy(bf16[48,8,64,128]{3,2,1,0:T(8,128)(2,1)S(1)} %bitcast.66) | data formatting | bytes 12582912 | tf_op jit(solution)/shard_map/while
  331.9 2.2 convolution_convert_fusion.4
  334.1 12.5 %copy.22 = bf16[48,8,64,128]{3,1,2,0:T(8,128)(2,1)S(1)} copy(bf16[48,8,64,128]{3,2,1,0:T(8,128)(2,1)S(1)} %bitcast.65) | data formatting | bytes 12582912 | tf_op jit(solution)/shard_map/while
  346.6 5.6 %fusion.68 = bf16[8192,256]{1,0:T(8,128)(2,1)S(1)} fusion(bf16[768,256]{1,0:T(8,128)(2,1)S(1)} %get-tuple-element.424, bf16[8192,384]{0,1:T(8,128)(2,1)S(1)} %bitcast.68, bf16[8192,384]{0,1:T(8,128)(2,1)S(1)} %bitcast.67), kind=kOutput, calls=%fused_computation.9.clone.1 | convolution fusion | flops 3248488448 | bytes 17170432 | tf_op jit(solution)/shard_map/while/body/eval_jaxpr/dot_general | solution.py:70
  352.2 2.3 constant_dynamic-update-slice_fusion.2
  354.4 0.6 dynamic_slice.69
  357.0 0.6 constant_dynamic-slice_fusion.9
  361.2 1.5 constant_dynamic-slice_fusion.10
  362.7 0.6 copy.20
  363.9 0.6 copy.21
  364.8 2.2 convolution_convert_fusion.5
  366.9 12.5 %copy.23 = bf16[48,8,64,128]{3,1,2,0:T(8,128)(2,1)S(1)} copy(bf16[48,8,64,128]{3,2,1,0:T(8,128)(2,1)S(1)} %bitcast.66) | data formatting | bytes 12582912 | tf_op jit(solution)/shard_map/while
  379.4 2.2 convolution_convert_fusion.4
  381.6 12.5 %copy.22 = bf16[48,8,64,128]{3,1,2,0:T(8,128)(2,1)S(1)} copy(bf16[48,8,64,128]{3,2,1,0:T(8,128)(2,1)S(1)} %bitcast.65) | data formatting | bytes 12582912 | tf_op jit(solution)/shard_map/while
  394.1 5.6 %fusion.68 = bf16[8192,256]{1,0:T(8,128)(2,1)S(1)} fusion(bf16[768,256]{1,0:T(8,128)(2,1)S(1)} %get-tuple-element.424, bf16[8192,384]{0,1:T(8,128)(2,1)S(1)} %bitcast.68, bf16[8192,384]{0,1:T(8,128)(2,1)S(1)} %bitcast.67), kind=kOutput, calls=%fused_computation.9.clone.1 | convolution fusion | flops 3248488448 | bytes 17170432 | tf_op jit(solution)/shard_map/while/body/eval_jaxpr/dot_general | solution.py:70
  399.6 2.3 constant_dynamic-update-slice_fusion.2
  (27 shorter events, 3.7 us)
Async XLA Ops:
  6.5 151.5 %all-gather.5.cloned.1.call-start = ((), (), s32[]{:S(2)}) async-start(), calls=%async_computation | async-start | bytes 3538944 | tf_op jit(solution)/shard_map/all_gather | solution.py:94
  7.9 58.9 %collective-permute-start = (bf16[128,4352]{1,0:T(8,128)(2,1)S(1)}, bf16[128,4352]{1,0:T(8,128)(2,1)}, u32[]{:S(2)}, u32[]{:S(2)}) collective-permute-start(bf16[128,4352]{1,0:T(8,128)(2,1)S(1)} %slice.29), channel_id=1, source_target_pairs={{16,0},{17,1},{18,2},{19,3},{20,4},{21,5},{22,6},{23,7},{24,8},{25... | collective-permute-start | bytes 3342344 | tf_op jit(solution)/shard_map/ppermute | solution.py:21
  61.8 5.0 %copy-start = (bf16[128,7680]{1,0:T(8,128)(2,1)S(1)}, bf16[128,7680]{1,0:T(8,128)(2,1)}, u32[]{:S(2)}) copy-start(bf16[128,7680]{1,0:T(8,128)(2,1)} %param.7) | copy-start | bytes 5898244
  61.8 6.4 %copy-start.2 = (s32[4]{0:T(128)S(1)}, s32[4]{0:T(128)}, u32[]{:S(2)}) copy-start(s32[4]{0:T(128)} %param.8) | copy-start | bytes 52
  68.2 122.6 %copy-start.1 = (s32[1,1,4,2]{2,3,1,0:T(2,128)S(1)}, s32[1,1,4,2]{2,3,1,0:T(2,128)}, u32[]{:S(2)}) copy-start(s32[1,1,4,2]{2,3,1,0:T(2,128)} %param.9) | copy-start | bytes 100
  93.1 97.7 %all-gather.7.cloned.1.call-start = ((), (), s32[]{:S(2)}) async-start(), calls=%async_computation.1 | async-start | bytes 3538944 | tf_op jit(solution)/shard_map/all_gather | solution.py:93
Sparse Core Ops, SparseCore 0:
  93.2 64.8 all-gather.4
  160.0 30.8 all-gather.6
where the time goes:
time: 415 us; the launch traced here: 409 us
  local copies, waits for them, and re-layouts  130 us (31%)
  waiting for transfers between devices  95.7 us (23%)
  other arithmetic  66.6 us (16%)
  matrix products  55.2 us (13%)
  loops' own time  46.9 us (11%)
  between operations  13.9 us (3%)
    while x8, local copies, waits for them, and re-layouts  99.7 us
    all_gather x1, waiting for transfers between devices, on_device(): col_gathered = lax.all_gather(own_piece, ('tm', 'prow'), axis=0, tiled=True)  62.2 us
    another operation x2, other arithmetic  54.4 us
    another operation x1, loops' own time, on_device(): result = lax.map(one_pair, jnp.arange(NP, dtype=jnp.int32))  43.2 us
    all_gather x1, waiting for transfers between devices, on_device(): row_gathered = lax.all_gather(own_piece, ('tm', 'pcol'), axis=0, tiled=True)  32.8 us
    dot_general x4, matrix products, cross_pair(): jnp.dot(flat, lags, preferred_element_type=jnp.float32).astype(jnp.bfloat16)  22.3 us
    dot_general x2, matrix products, one_window(): return jnp.dot(segment, dft_table, preferred_element_type=jnp.float32)  13.9 us
    dynamic_update_slice x4, local copies, waits for them, and re-layouts, on_device(): result = lax.map(one_pair, jnp.arange(NP, dtype=jnp.int32))  9.16 us
  transfers between devices with their start and end apart: 3, of which 2 were waited for; matrix products, arithmetic and copies ran while one was open for 15% of the time, Pallas kernels for 0%

commit v1 on v0

--- a/solution.py
+++ b/solution.py
@@ -13,6 +13,18 @@
 STEP = 3840
 HALO = 4352
 two_pi = 2.0 * math.pi
+
+
+def gather_by_bits(x, axis, dim):
+    ways, here = (lax.axis_size(axis), lax.axis_index(axis))
+    grown, reach = (x, 1)
+    while reach < ways:
+        theirs = lax.ppermute(grown, axis, [(d, d ^ reach) for d in range(ways)])
+        mine_first = jnp.concatenate([grown, theirs], axis=dim)
+        theirs_first = jnp.concatenate([theirs, grown], axis=dim)
+        grown = jnp.where(here & reach == 0, mine_first, theirs_first)
+        reach = 2 * reach
+    return grown
 
 
 def from_behind(value, axis, steps):
@@ -90,7 +102,7 @@
     spectra = lax.map(one_window, jnp.arange(w_dev, dtype=jnp.int32))
     whitened = whiten(spectra)
     own_piece = whitened[None]
-    row_gathered = lax.all_gather(own_piece, ("tm", "pcol"), axis=0, tiled=True)
+    row_gathered = gather_by_bits(own_piece, ("tm", "pcol"), 0)
     col_gathered = lax.all_gather(own_piece, ("tm", "prow"), axis=0, tiled=True)
     row_gathered = row_gathered.reshape(n_tm, -1, w_dev, channels_here, 2 * NF)
     col_gathered = col_gathered.reshape(n_tm, -1, w_dev, channels_here, 2 * NF)

time: 415 us -> 400 us (0.964)
  waiting for transfers between devices: 95.7 us -> 69.6 us
  starting transfers between devices: 1.34 us -> 8.45 us
    ppermute x0 -> x3, waiting for transfers between devices: none -> 68.5 us  [gather_by_bits(): theirs = lax.ppermute(grown, axis, [(d, d ^ reach) for d in range(ways)])]
    all_gather x1, waiting for transfers between devices: 62.2 us -> 1.07 us  [on_device(): col_gathered = lax.all_gather(own_piece, ('tm', 'prow'), axis=0, tiled=True)]
    all_gather x1 -> x0, waiting for transfers between devices: 32.8 us -> none  [on_device(): row_gathered = lax.all_gather(own_piece, ('tm', 'pcol'), axis=0, tiled=True)]
    ppermute x0 -> x3, starting transfers between devices: none -> 7.16 us  [gather_by_bits(): theirs = lax.ppermute(grown, axis, [(d, d ^ reach) for d in range(ways)])]
  transfers between devices with their start and end apart: 3 -> 5, of which waited for: 2 -> 4; matrix products, arithmetic and copies ran while one was open for 15% -> 16% of each run, Pallas kernels for 0% -> 0%
where the time goes in v1:
time: 400 us; the launch traced here: 393 us
  local copies, waits for them, and re-layouts  130 us (32%)
  other arithmetic  70 us (18%)
  waiting for transfers between devices  69.6 us (17%)
  matrix products  55.1 us (14%)
  loops' own time  46.9 us (12%)
  between operations  13.9 us (3%)
  starting transfers between devices  8.45 us (2%)
    while x8, local copies, waits for them, and re-layouts  99.7 us
    ppermute x3, waiting for transfers between devices, gather_by_bits(): theirs = lax.ppermute(grown, axis, [(d, d ^ reach) for d in range(ways)])  68.5 us
    another operation x2, other arithmetic  54.4 us
    another operation x1, loops' own time, on_device(): result = lax.map(one_pair, jnp.arange(NP, dtype=jnp.int32))  43.2 us
    dot_general x4, matrix products, cross_pair(): jnp.dot(flat, lags, preferred_element_type=jnp.float32).astype(jnp.bfloat16)  22.2 us
    dot_general x2, matrix products, one_window(): return jnp.dot(segment, dft_table, preferred_element_type=jnp.float32)  13.9 us
    dynamic_update_slice x4, local copies, waits for them, and re-layouts, on_device(): result = lax.map(one_pair, jnp.arange(NP, dtype=jnp.int32))  9.16 us
    dot_general x4, matrix products, cross_pair(): jnp.einsum('wif,wjf->ijf', row_second, col_both, preferred_element_type=j...  8.64 us
  transfers between devices with their start and end apart: 5, of which 4 were waited for; matrix products, arithmetic and copies ran while one was open for 16% of the time, Pallas kernels for 0%

profile of v1, /device:TPU:0, one launch (start us, length us, event | category | flops | bytes accessed | tf_op | source)
XLA Modules:
  0.0 393.5 jit_solution(9847121963589465245)
XLA Ops:
  6.5 1.3 slice.29
  7.9 1.3 collective-permute-start
  9.3 52.4 %multiply_convert_fusion.1 = (bf16[7680,384]{1,0:T(8,128)(2,1)S(1)}, bf16[7680,384]{1,0:T(8,128)(2,1)S(1)}) fusion(s32[384]{0:T(512)S(1)} %iota_add_fusion, f32[7680]{0:T(1024)S(1)} %get-tuple-element.245, f32[7680]{0:T(1024)S(1)} %get-tuple-element.246), kind=kLoop, calls=%fused_computation.36 | loop fusion | flops 38338560 | bytes 11859456 | tf_op jit(solution)/shard_map/convert.8
  61.8 5.0 %pad_maximum_fusion.3 = bf16[7680,768]{1,0:T(8,128)(2,1)} fusion(bf16[7680,384]{1,0:T(8,128)(2,1)S(1)} %get-tuple-element.244, bf16[7680,384]{1,0:T(8,128)(2,1)S(1)} %get-tuple-element.243), kind=kLoop, calls=%fused_computation.34 | loop fusion | flops 23592960 | bytes 23592960 | tf_op jit(solution)/shard_map/concatenate | solution.py:44
  66.7 1.5 pad_maximum_fusion.4
  68.2 19.9 %while.24 = (s32[]{:T(128)}, f32[2,128,768]{2,1,0:T(8,128)}, s32[2]{0:T(128)S(1)}, s32[]{:T(128)}, s32[4]{0:T(128)S(1)}, /*index=5*/bf16[128,12032]{1,0:T(8,128)...) while((s32[]{:T(128)}, f32[2,128,768]{2,1,0:T(8,128)}, ...), condition=%wide.region_1.2_spmd, body=%wide.region_0.1_spmd.sunk | while | flops 1509949440 | bytes 14156537 | solution.py:102
  68.2 0.6 dynamic_slice.65
  71.2 7.0 %fusion.61 = f32[2,128,768]{2,1,0:T(8,128)} fusion(f32[2,128,768]{2,1,0:T(8,128)} %get-tuple-element.370, s32[]{:T(128)} %get-tuple-element.369, bf16[7680,768]{1,0:T(8,128)(2,1)} %get-tuple-element.387, bf16[128,12032]{1,0:T(8,128)(2,1)S(1)} %get-tuple-element.386, s32[]{:T(128)S(6)} %select_n.131), kind=kOutput, calls=%fused_computation.3.clone.1 | convolution fusion | flops 1509949440 | bytes 14156292 | tf_op jit(solution)/shard_map/while/body/eval_jaxpr/dot_general | solution.py:100
  78.2 0.6 dynamic_slice.65
  81.2 6.9 %fusion.61 = f32[2,128,768]{2,1,0:T(8,128)} fusion(f32[2,128,768]{2,1,0:T(8,128)} %get-tuple-element.370, s32[]{:T(128)} %get-tuple-element.369, bf16[7680,768]{1,0:T(8,128)(2,1)} %get-tuple-element.387, bf16[128,12032]{1,0:T(8,128)(2,1)S(1)} %get-tuple-element.386, s32[]{:T(128)S(6)} %select_n.131), kind=kOutput, calls=%fused_computation.3.clone.1 | convolution fusion | flops 1509949440 | bytes 14156292 | tf_op jit(solution)/shard_map/while/body/eval_jaxpr/dot_general | solution.py:100
  88.1 1.2 fusion.42
  89.4 1.7 fusion.32
  91.1 2.0 fusion.33
  93.6 1.6 collective-permute-done.1
  95.2 1.2 maximum_select_fusion.2
  96.4 3.0 collective-permute-start.2
  99.4 17.8 %collective-permute-done.2 = bf16[2,2,128,768]{3,2,1,0:T(8,128)(2,1)S(1)} collective-permute-done((bf16[2,2,128,768]{3,2,1,0:T(8,128)(2,1)S(1)}, bf16[2,2,128,768]{3,2,1,0:T(8,128)(2,1)S(1)}, u32[]{:S(2)}, u32[]{:S(2)}) %collective-permute-start.2) | collective-permute-done | bytes 786464 | tf_op jit(solution)/shard_map/ppermute | solution.py:22
  117.5 3.6 collective-permute-start.3
  121.1 1.9 multiply_convert_fusion.3
  123.1 49.1 %collective-permute-done.3 = bf16[4,2,128,768]{3,2,1,0:T(8,128)(2,1)S(1)} collective-permute-done((bf16[4,2,128,768]{3,2,1,0:T(8,128)(2,1)S(1)}, bf16[4,2,128,768]{3,2,1,0:T(8,128)(2,1)S(1)}, u32[]{:S(2)}, u32[]{:S(2)}) %collective-permute-start.3) | collective-permute-done | bytes 1572896 | tf_op jit(solution)/shard_map/ppermute | solution.py:22
  172.2 1.9 maximum_select_fusion
  174.1 1.1 all-gather.3.cloned.1.call-done
  175.2 211.0 %while.25 = (s32[]{:T(128)}, bf16[4,64,128,256]{3,2,1,0:T(8,128)(2,1)}, s32[4]{0:T(128)S(1)}, s32[4,2]{0,1:T(2,128)S(1)}, bf16[2,4,2,128,768]{4,3,2,1,0:T(8,128)...) while((s32[]{:T(128)}, ...), condition=%wide.region_4.5_spmd, body=%wide.region_3.4_spmd.sunk | while | flops 3360456704 | bytes 74515224 | solution.py:125
  196.3 0.6 dynamic_slice.69
  198.8 0.6 constant_dynamic-slice_fusion.9
  203.1 1.5 constant_dynamic-slice_fusion.10
  204.6 0.6 copy.20
  205.8 0.6 copy.21
  206.7 2.2 convolution_convert_fusion.5
  208.8 12.5 %copy.23 = bf16[48,8,64,128]{3,1,2,0:T(8,128)(2,1)S(1)} copy(bf16[48,8,64,128]{3,2,1,0:T(8,128)(2,1)S(1)} %bitcast.67) | data formatting | bytes 12582912 | tf_op jit(solution)/shard_map/while
  221.3 2.2 convolution_convert_fusion.4
  223.5 12.5 %copy.22 = bf16[48,8,64,128]{3,1,2,0:T(8,128)(2,1)S(1)} copy(bf16[48,8,64,128]{3,2,1,0:T(8,128)(2,1)S(1)} %bitcast.66) | data formatting | bytes 12582912 | tf_op jit(solution)/shard_map/while
  236.0 5.6 %fusion.68 = bf16[8192,256]{1,0:T(8,128)(2,1)S(1)} fusion(bf16[768,256]{1,0:T(8,128)(2,1)S(1)} %get-tuple-element.424, bf16[8192,384]{0,1:T(8,128)(2,1)S(1)} %bitcast.69, bf16[8192,384]{0,1:T(8,128)(2,1)S(1)} %bitcast.68), kind=kOutput, calls=%fused_computation.9.clone.1 | convolution fusion | flops 3248488448 | bytes 17170432 | tf_op jit(solution)/shard_map/while/body/eval_jaxpr/dot_general | solution.py:82
  241.5 2.3 constant_dynamic-update-slice_fusion.2
  243.8 0.6 dynamic_slice.69
  246.3 0.6 constant_dynamic-slice_fusion.9
  250.6 1.5 constant_dynamic-slice_fusion.10
  252.1 0.6 copy.20
  254.1 2.2 convolution_convert_fusion.5
  256.3 12.5 %copy.23 = bf16[48,8,64,128]{3,1,2,0:T(8,128)(2,1)S(1)} copy(bf16[48,8,64,128]{3,2,1,0:T(8,128)(2,1)S(1)} %bitcast.67) | data formatting | bytes 12582912 | tf_op jit(solution)/shard_map/while
  268.8 2.2 convolution_convert_fusion.4
  271.0 12.5 %copy.22 = bf16[48,8,64,128]{3,1,2,0:T(8,128)(2,1)S(1)} copy(bf16[48,8,64,128]{3,2,1,0:T(8,128)(2,1)S(1)} %bitcast.66) | data formatting | bytes 12582912 | tf_op jit(solution)/shard_map/while
  283.4 5.6 %fusion.68 = bf16[8192,256]{1,0:T(8,128)(2,1)S(1)} fusion(bf16[768,256]{1,0:T(8,128)(2,1)S(1)} %get-tuple-element.424, bf16[8192,384]{0,1:T(8,128)(2,1)S(1)} %bitcast.69, bf16[8192,384]{0,1:T(8,128)(2,1)S(1)} %bitcast.68), kind=kOutput, calls=%fused_computation.9.clone.1 | convolution fusion | flops 3248488448 | bytes 17170432 | tf_op jit(solution)/shard_map/while/body/eval_jaxpr/dot_general | solution.py:82
  289.0 2.3 constant_dynamic-update-slice_fusion.2
  291.3 0.6 dynamic_slice.69
  293.8 0.6 constant_dynamic-slice_fusion.9
  298.0 1.5 constant_dynamic-slice_fusion.10
  301.6 2.2 convolution_convert_fusion.5
  303.8 12.5 %copy.23 = bf16[48,8,64,128]{3,1,2,0:T(8,128)(2,1)S(1)} copy(bf16[48,8,64,128]{3,2,1,0:T(8,128)(2,1)S(1)} %bitcast.67) | data formatting | bytes 12582912 | tf_op jit(solution)/shard_map/while
  316.3 2.2 convolution_convert_fusion.4
  318.4 12.5 %copy.22 = bf16[48,8,64,128]{3,1,2,0:T(8,128)(2,1)S(1)} copy(bf16[48,8,64,128]{3,2,1,0:T(8,128)(2,1)S(1)} %bitcast.66) | data formatting | bytes 12582912 | tf_op jit(solution)/shard_map/while
  330.9 5.6 %fusion.68 = bf16[8192,256]{1,0:T(8,128)(2,1)S(1)} fusion(bf16[768,256]{1,0:T(8,128)(2,1)S(1)} %get-tuple-element.424, bf16[8192,384]{0,1:T(8,128)(2,1)S(1)} %bitcast.69, bf16[8192,384]{0,1:T(8,128)(2,1)S(1)} %bitcast.68), kind=kOutput, calls=%fused_computation.9.clone.1 | convolution fusion | flops 3248488448 | bytes 17170432 | tf_op jit(solution)/shard_map/while/body/eval_jaxpr/dot_general | solution.py:82
  336.5 2.3 constant_dynamic-update-slice_fusion.2
  338.8 0.6 dynamic_slice.69
  341.3 0.6 constant_dynamic-slice_fusion.9
  345.5 1.5 constant_dynamic-slice_fusion.10
  347.0 0.6 copy.20
  348.2 0.6 copy.21
  349.1 2.2 convolution_convert_fusion.5
  351.3 12.5 %copy.23 = bf16[48,8,64,128]{3,1,2,0:T(8,128)(2,1)S(1)} copy(bf16[48,8,64,128]{3,2,1,0:T(8,128)(2,1)S(1)} %bitcast.67) | data formatting | bytes 12582912 | tf_op jit(solution)/shard_map/while
  363.7 2.2 convolution_convert_fusion.4
  365.9 12.5 %copy.22 = bf16[48,8,64,128]{3,1,2,0:T(8,128)(2,1)S(1)} copy(bf16[48,8,64,128]{3,2,1,0:T(8,128)(2,1)S(1)} %bitcast.66) | data formatting | bytes 12582912 | tf_op jit(solution)/shard_map/while
  378.4 5.6 %fusion.68 = bf16[8192,256]{1,0:T(8,128)(2,1)S(1)} fusion(bf16[768,256]{1,0:T(8,128)(2,1)S(1)} %get-tuple-element.424, bf16[8192,384]{0,1:T(8,128)(2,1)S(1)} %bitcast.69, bf16[8192,384]{0,1:T(8,128)(2,1)S(1)} %bitcast.68), kind=kOutput, calls=%fused_computation.9.clone.1 | convolution fusion | flops 3248488448 | bytes 17170432 | tf_op jit(solution)/shard_map/while/body/eval_jaxpr/dot_general | solution.py:82
  383.9 2.3 constant_dynamic-update-slice_fusion.2
  (33 shorter events, 7.4 us)
Async XLA Ops:
  6.5 168.7 %all-gather.3.cloned.1.call-start = ((), (), s32[]{:S(2)}) async-start(), calls=%async_computation | async-start | bytes 3538944 | tf_op jit(solution)/shard_map/all_gather | solution.py:106
  7.9 58.9 %collective-permute-start = (bf16[128,4352]{1,0:T(8,128)(2,1)S(1)}, bf16[128,4352]{1,0:T(8,128)(2,1)}, u32[]{:S(2)}, u32[]{:S(2)}) collective-permute-start(bf16[128,4352]{1,0:T(8,128)(2,1)S(1)} %slice.29), channel_id=1, source_target_pairs={{16,0},{17,1},{18,2},{19,3},{20,4},{21,5},{22,6},{23,7},{24,8},{25... | collective-permute-start | bytes 3342344 | tf_op jit(solution)/shard_map/ppermute | solution.py:33
  61.8 5.0 %copy-start = (bf16[128,7680]{1,0:T(8,128)(2,1)S(1)}, bf16[128,7680]{1,0:T(8,128)(2,1)}, u32[]{:S(2)}) copy-start(bf16[128,7680]{1,0:T(8,128)(2,1)} %param.7) | copy-start | bytes 5898244
  66.7 1.5 copy-start.2
  93.1 2.1 collective-permute-start.1
  93.6 81.6 %copy-start.1 = (s32[1,1,4,2]{2,3,1,0:T(2,128)S(1)}, s32[1,1,4,2]{2,3,1,0:T(2,128)}, u32[]{:S(2)}) copy-start(s32[1,1,4,2]{2,3,1,0:T(2,128)} %param.9) | copy-start | bytes 100
  96.4 20.8 %collective-permute-start.2 = (bf16[2,2,128,768]{3,2,1,0:T(8,128)(2,1)S(1)}, bf16[2,2,128,768]{3,2,1,0:T(8,128)(2,1)S(1)}, u32[]{:S(2)}, u32[]{:S(2)}) collective-permute-start(bf16[2,2,128,768]{3,2,1,0:T(8,128)(2,1)S(1)} %maximum_select_fusion.2), channel_id=1, source_target_pairs={{0,2},{1,3},{2,0},{3,1},{16,18},{17,19},{18,16},{19,17},{4,6},{5,7... | collective-permute-start | bytes 2359304 | tf_op jit(solution)/shard_map/ppermute | solution.py:22
  117.5 54.7 %collective-permute-start.3 = (bf16[4,2,128,768]{3,2,1,0:T(8,128)(2,1)S(1)}, bf16[4,2,128,768]{3,2,1,0:T(8,128)(2,1)S(1)}, u32[]{:S(2)}, u32[]{:S(2)}) collective-permute-start(bf16[4,2,128,768]{3,2,1,0:T(8,128)(2,1)S(1)} %maximum_select_fusion.1), channel_id=1, source_target_pairs={{0,16},{1,17},{2,18},{3,19},{16,0},{17,1},{18,2},{19,3},{4,20},{5,... | collective-permute-start | bytes 4718600 | tf_op jit(solution)/shard_map/ppermute | solution.py:22
Sparse Core Ops, SparseCore 0:
  93.2 81.9 all-gather.2
